TPU v7x, 512 devices: a whole 4x8x8 slice. The times are simulated.
512 devices in a mesh: pipe: 32 (over y, z_lo), seq: 16 (over z_hi, x, core).
Axes of the slice: x: 4, y: 8, z: 8 (z_hi: 2, z_lo: 4; z = z_hi * 4 + z_lo), core: 2. Of those that a mesh axis runs over, the one named last changes fastest.
Arguments:
- x_first: bfloat16 [4096, 2560], P(('pipe', 'seq')), may hold values from -6 to 6
- x_second: bfloat16 [4096, 2560], P(('pipe', 'seq')), may hold values from -6 to 6
- stale_kv: bfloat16 [2, 4096, 2048], P(None, 'pipe', 'seq'), may hold values from -6 to 6
- w_qkv: bfloat16 [3, 2560, 2048], P(None, None, 'seq'), may hold values from -0.125 to 0.125
- w_out: bfloat16 [2048, 2560], P('seq'), may hold values from -0.125 to 0.125
- q_gain: float32 [2048], P('seq'), may hold values from 0.4 to 5
- k_gain: float32 [2048], P('seq'), may hold values from 0.4 to 5
- layout: int32 [32, 16], replicated, may hold values from 0 to 31, as said below
- counts: int32 [32], replicated, may hold values from 1 to 16, as said below
- slot_block: int32 [32], replicated, may hold values from 0 to 31, each once
Outputs:
- out_first: bfloat16 [4096, 2560], P(('pipe', 'seq'))
- out_second: bfloat16 [4096, 2560], P(('pipe', 'seq'))
Inputs may be any that keep to these rules, and one draw needn't show every extreme that they name: `layout`: entries of a row are distinct sequence blocks and the first entry of row b is b itself. `counts`: some block reads 16 entries. `slot_block`: each block once.
All inputs are finite; a program needn't handle non-finite values.
Results may differ from a plain program's by a relative error of at most 0.019.
Values may be sent and summed in bfloat16 or wider, within the bound.
No kernel may reach another device: no remote copies, remote signals or barrier semaphores. Data moves between devices by JAX's collectives and lax.ppermute only.
A program may use at most 64 MiB of HBM per device.

v0:
```python
import math
import jax
import jax.numpy as jnp
from jax import lax
from jax.sharding import PartitionSpec as P

HS = 64
BLOCK = 128
BPM = 1
HIGH = lax.Precision.HIGHEST
NEG = -1e30


def slot_mask(layout, counts, slot_block):
    total = layout.shape[0]
    width = layout.shape[1]
    blocks = jnp.arange(total, dtype=jnp.int32)
    valid = jnp.arange(width, dtype=jnp.int32)[None, :] < counts[:, None]
    member = jnp.sum(
        ((layout[:, :, None] == blocks[None, None, :]) & valid[:, :, None]).astype(jnp.float32),
        axis=1,
    )
    placed = (slot_block[:, None] == blocks[None, :]).astype(jnp.float32)
    linked = jnp.dot(jnp.dot(placed, member, precision=HIGH), placed.T, precision=HIGH)
    return linked > 0.5


def normalize(raw, gain, size):
    count = raw.shape[0]
    grid = raw.reshape(count, -1, size)
    factor = lax.rsqrt(jnp.mean(grid * grid, axis=2, keepdims=True) + 1e-06)
    return (grid * factor).reshape(count, -1) * gain[None, :]


def partial_attend(query, keys, values, allowed, scale):
    heads = query.shape[1]
    qrows = query.shape[0]
    krows = keys.shape[0]
    scores = jnp.einsum("qhd,khd->hqk", query, keys, preferred_element_type=jnp.float32) * scale
    grid = scores.reshape(heads, qrows // BLOCK, BLOCK, krows // BLOCK, BLOCK)
    keep = allowed[None, :, None, :, None]
    grid = jnp.where(keep, grid, NEG)
    top = jnp.max(grid, axis=(3, 4))
    weights = jnp.where(keep, jnp.exp(grid - top[:, :, :, None, None]), 0.0)
    total = jnp.sum(weights, axis=(3, 4))
    weights = weights.reshape(heads, qrows, krows)
    summed = jnp.einsum("hqk,khd->qhd", weights, values.astype(jnp.float32), precision=HIGH)
    return (top.reshape(heads, qrows), total.reshape(heads, qrows), summed)


def merge_parts(first, second):
    top_a, total_a, summed_a = first
    top_b, total_b, summed_b = second
    best = jnp.maximum(top_a, top_b)
    keep_a = jnp.exp(top_a - best)
    keep_b = jnp.exp(top_b - best)
    merged = summed_a * keep_a.T[:, :, None] + summed_b * keep_b.T[:, :, None]
    return (best, total_a * keep_a + total_b * keep_b, merged)


def on_device(
    x_first, x_second, stale_kv, w_qkv, w_out, q_gain, k_gain, layout, counts, slot_block
):
    me = lax.axis_index("pipe")
    tokens = BPM * BLOCK
    heads = w_qkv.shape[2] // HS
    width = heads * HS
    scale = 1.0 / math.sqrt(HS)
    linked = slot_mask(layout, counts, slot_block)
    total_blocks = linked.shape[0]
    block_ids = jnp.arange(total_blocks, dtype=jnp.int32)
    batch_of = block_ids // BPM
    mine = lax.dynamic_slice_in_dim(linked, me * BPM, BPM, 0)
    own = lax.dynamic_slice_in_dim(mine, me * BPM, BPM, 1)
    remote = mine & (batch_of != me)[None, :]

    def step(x_rows, prior_k, prior_v):
        raw = jnp.einsum(
            "rd,cdh->crh",
            lax.all_gather(x_rows, "seq", axis=0, tiled=True),
            w_qkv,
            preferred_element_type=jnp.float32,
        )
        query = normalize(raw[0], q_gain, HS).astype(jnp.bfloat16)
        keys = normalize(raw[1], k_gain, HS).astype(jnp.bfloat16)
        values = raw[2].astype(jnp.bfloat16)
        query_h = query.reshape(tokens, heads, HS)
        start_part = partial_attend(
            query_h, keys.reshape(tokens, heads, HS), values.reshape(tokens, heads, HS), own, scale
        )
        piece_k = lax.all_gather(prior_k, "pipe", axis=0, tiled=True)
        piece_v = lax.all_gather(prior_v, "pipe", axis=0, tiled=True)
        count = piece_k.shape[0]
        fresh = partial_attend(
            query_h,
            piece_k.reshape(count, heads, HS),
            piece_v.reshape(count, heads, HS),
            remote,
            scale,
        )
        best, denom_h, numer = merge_parts(start_part, fresh)
        denom = denom_h.T
        attn = (numer / denom[:, :, None]).reshape(tokens, width).astype(jnp.bfloat16)
        out = lax.psum_scatter(
            jnp.dot(attn, w_out, preferred_element_type=jnp.float32).astype(jnp.bfloat16),
            "seq",
            scatter_dimension=0,
            tiled=True,
        )
        return (out, keys, values)

    out_first, keys_first, values_first = step(x_first, stale_kv[0], stale_kv[1])
    out_second, unused_k, unused_v = step(x_second, keys_first, values_first)
    return (out_first, out_second)


def solution(mesh):
    placed = (
        P(("pipe", "seq"), None),
        P(("pipe", "seq"), None),
        P(None, "pipe", "seq"),
        P(None, None, "seq"),
        P("seq", None),
        P("seq"),
        P("seq"),
        P(),
        P(),
        P(),
    )
    return jax.shard_map(
        on_device,
        mesh=mesh,
        in_specs=placed,
        out_specs=(P(("pipe", "seq"), None), P(("pipe", "seq"), None)),
        check_vma=False,
    )
```

profile of v0, /device:TPU:8, one launch (start us, length us, event | category | flops | bytes accessed | tf_op | source)
XLA Modules:
  0.0 786.6 jit_solution(18196252297809986685)
XLA Ops:
  7.3 37.1 %all_gather.18 = bf16[128,2560]{1,0:T(8,128)(2,1)S(1)} all-gather(bf16[8,2560]{1,0:T(8,128)(2,1)} %param.10), channel_id=1, replica_groups=mesh['pipe'=32,'seq'=16] {'seq'}, dimensions={0}, use_global_device_ids=true | all-gather | bytes 696320 | tf_op jit(solution)/shard_map/all_gather | solution.py:80
  45.2 1.3 fusion.32
  46.6 1.4 fusion.62
  49.5 27.8 %all_gather.21 = bf16[128,2560]{1,0:T(8,128)(2,1)S(1)} all-gather(bf16[8,2560]{1,0:T(8,128)(2,1)S(1)} %copy-done.5), channel_id=1, replica_groups=mesh['pipe'=32,'seq'=16] {'seq'}, dimensions={0}, use_global_device_ids=true | all-gather | bytes 696320 | tf_op jit(solution)/shard_map/all_gather | solution.py:80
  79.8 1.0 fusion.65
  80.8 1.0 fusion.66
  82.5 85.6 %all-gather.8.cloned.1.call-done = bf16[4096,128]{0,1:T(8,128)(2,1)} async-done(((bf16[128,128]{0,1:T(8,128)(2,1)}), bf16[4096,128]{0,1:T(8,128)(2,1)}) %all-gather.8.cloned.1.call-update) | async-done | bytes 1048592 | tf_op jit(solution)/shard_map/all_gather | solution.py:91
  168.1 4.0 fusion.64
  172.1 144.8 %all-gather.10.cloned.1.call-done = bf16[1,4096,128]{2,1,0:T(8,128)(2,1)} async-done(((bf16[1,128,128]{2,1,0:T(8,128)(2,1)}), bf16[1,4096,128]{2,1,0:T(8,128)(2,1)}) %all-gather.10.cloned.1.call-update) | async-done | bytes 1048592 | tf_op jit(solution)/shard_map/all_gather | solution.py:91
  317.0 1.5 copy.22
  318.5 0.9 fusion.63
  319.4 1.9 copy-done.1
  321.4 1.6 fusion.4
  323.0 124.8 %all-gather.14.cloned.1.call-done = bf16[1,4096,128]{1,2,0:T(8,128)(2,1)} async-done(((bf16[1,128,128]{1,2,0:T(8,128)(2,1)}), bf16[1,4096,128]{1,2,0:T(8,128)(2,1)}) %all-gather.14.cloned.1.call-update) | async-done | bytes 1048592 | tf_op jit(solution)/shard_map/all_gather | solution.py:92
  447.9 5.6 fusion.23
  453.5 0.9 fusion.24
  454.4 1.2 convolution_convert_fusion
  455.8 140.8 %all-gather.12.cloned.1.call-done = bf16[1,4096,128]{2,1,0:T(8,128)(2,1)} async-done(((bf16[1,128,128]{2,1,0:T(8,128)(2,1)}), bf16[1,4096,128]{2,1,0:T(8,128)(2,1)}) %all-gather.12.cloned.1.call-update) | async-done | bytes 1048592 | tf_op jit(solution)/shard_map/all_gather | solution.py:92
  596.7 2.3 copy.23
  599.0 5.5 fusion.22
  604.5 0.9 fusion.25
  605.4 1.2 convolution_convert_fusion.1
  606.6 85.7 %reduce-scatter.5.cloned.1.call-done = bf16[8,2560]{1,0:T(8,128)(2,1)} async-done(((bf16[128,2560]{1,0:T(8,128)(2,1)}), bf16[8,2560]{1,0:T(8,128)(2,1)}) %reduce-scatter.5.cloned.1.call-update) | async-done | bytes 40976 | tf_op jit(solution)/shard_map/reduce_scatter | solution.py:104
  692.3 87.4 %reduce-scatter.3.cloned.1.call-done = bf16[8,2560]{1,0:T(8,128)(2,1)} async-done(((bf16[128,2560]{1,0:T(8,128)(2,1)}), bf16[8,2560]{1,0:T(8,128)(2,1)}) %reduce-scatter.3.cloned.1.call-update) | async-done | bytes 40976 | tf_op jit(solution)/shard_map/reduce_scatter | solution.py:104
  (60 shorter events, 5.8 us)
Async XLA Ops:
  7.2 37.2 %copy-start = (bf16[3,2560,128]{2,1,0:T(8,128)(2,1)S(1)}, bf16[3,2560,128]{2,1,0:T(8,128)(2,1)}, u32[]{:S(2)}) copy-start(bf16[3,2560,128]{2,1,0:T(8,128)(2,1)} %param.13) | copy-start | bytes 5898244
  7.2 42.2 %copy-start.7 = (f32[128]{0:T(128)S(1)}, f32[128]{0:T(128)}, u32[]{:S(2)}) copy-start(f32[128]{0:T(128)} %param.16) | copy-start | bytes 1540
  7.2 42.3 %copy-start.5 = (bf16[8,2560]{1,0:T(8,128)(2,1)S(1)}, bf16[8,2560]{1,0:T(8,128)(2,1)}, u32[]{:S(2)}) copy-start(bf16[8,2560]{1,0:T(8,128)(2,1)} %param.11) | copy-start | bytes 122884
  7.2 70.9 %copy-start.6 = (s32[32,16]{0,1:T(8,128)S(1)}, s32[32,16]{0,1:T(8,128)}, u32[]{:S(2)}) copy-start(s32[32,16]{0,1:T(8,128)} %param.17) | copy-start | bytes 6148
  7.2 70.9 %copy-start.8 = (s32[32]{0:T(128)S(1)}, s32[32]{0:T(128)}, u32[]{:S(2)}) copy-start(s32[32]{0:T(128)} %param.18) | copy-start | bytes 388
  7.2 71.2 %copy-start.9 = (s32[32]{0:T(128)S(1)}, s32[32]{0:T(128)}, u32[]{:S(2)}) copy-start(s32[32]{0:T(128)} %param.19) | copy-start | bytes 388
  7.2 72.4 %copy-start.10 = (f32[128]{0:T(128)S(1)}, f32[128]{0:T(128)}, u32[]{:S(2)}) copy-start(f32[128]{0:T(128)} %param.15) | copy-start | bytes 1540
  7.2 160.8 %all-gather.8.cloned.1.call-start = ((), (), s32[]{:S(2)}) async-start(), calls=%async_computation.3 | async-start | bytes 1081344 | tf_op jit(solution)/shard_map/all_gather | solution.py:91
  46.5 270.4 %all-gather.10.cloned.1.call-start = ((), (), s32[]{:S(2)}) async-start(), calls=%async_computation.5 | async-start | bytes 1081344 | tf_op jit(solution)/shard_map/all_gather | solution.py:91
  48.0 399.9 %all-gather.14.cloned.1.call-start = ((), (), s32[]{:S(2)}) async-start(), calls=%async_computation.7 | async-start | bytes 1081344 | tf_op jit(solution)/shard_map/all_gather | solution.py:92
  48.8 547.9 %all-gather.12.cloned.1.call-start = ((), (), s32[]{:S(2)}) async-start(), calls=%async_computation.6 | async-start | bytes 1081344 | tf_op jit(solution)/shard_map/all_gather | solution.py:92
  49.3 642.9 %reduce-scatter.5.cloned.1.call-start = ((), (), s32[]{:S(2)}) async-start(), calls=%async_computation.4 | async-start | bytes 696320 | tf_op jit(solution)/shard_map/reduce_scatter | solution.py:104
  318.5 2.9 copy-start.1
  319.4 3.6 copy-start.2
  323.0 131.3 %copy-start.3 = (bf16[128,2560]{1,0:T(8,128)(2,1)S(1)}, bf16[128,2560]{1,0:T(8,128)(2,1)}, u32[]{:S(2)}) copy-start(bf16[128,2560]{1,0:T(8,128)(2,1)} %param.14) | copy-start | bytes 1966084
  455.6 148.9 %copy-start.4 = (bf16[1,128,128]{1,2,0:T(8,128)(2,1)S(1)}, bf16[1,128,128]{1,2,0:T(8,128)(2,1)}, u32[]{:S(2)}) copy-start(bf16[1,128,128]{1,2,0:T(8,128)(2,1)} %slice.43) | copy-start | bytes 98308
  455.6 324.1 %reduce-scatter.3.cloned.1.call-start = ((), (), s32[]{:S(2)}) async-start(), calls=%async_computation.2 | async-start | bytes 696320 | tf_op jit(solution)/shard_map/reduce_scatter | solution.py:104
Sparse Core Ops, SparseCore 0:
  46.7 121.3 all-gather.7
  170.7 146.1 all-gather.9
  319.0 128.8 all-gather.13
  450.4 146.2 all-gather.11
  601.7 90.4 reduce-scatter.4
  697.3 82.3 reduce-scatter.2
where the time goes:
time: 787 us
  waiting for transfers between devices  670 us (85%)
  blocking collectives  64.9 us (8%)
  matrix products  24 us (3%)
  between operations  14.4 us (2%)
  local copies, waits for them, and re-layouts  8.75 us (1%)
    all_gather x2, waiting for transfers between devices, step(): piece_v = lax.all_gather(prior_v, 'pipe', axis=0, tiled=True)  266 us
    all_gather x2, waiting for transfers between devices, step(): piece_k = lax.all_gather(prior_k, 'pipe', axis=0, tiled=True)  230 us
    reduce_scatter x2, waiting for transfers between devices, step(): lax.psum_scatter(jnp.dot(attn, w_out, preferred_element_type=jnp.float32)...  173 us
    all_gather x2, blocking collectives, step(): lax.all_gather(x_rows, 'seq', axis=0, tiled=True)  64.9 us
  transfers between devices with their start and end apart: 6, of which 6 were waited for; matrix products, arithmetic and copies ran while one was open for 4% of the time, Pallas kernels for 0%

commit v1 on v0

--- a/solution.py
+++ b/solution.py
@@ -88,7 +88,9 @@
         start_part = partial_attend(
             query_h, keys.reshape(tokens, heads, HS), values.reshape(tokens, heads, HS), own, scale
         )
-        piece_k = lax.all_gather(prior_k, "pipe", axis=0, tiled=True)
+        piece_k = jnp.concatenate(
+            lax.all_to_all(jnp.stack([prior_k] * lax.axis_size("pipe")), "pipe", 0, 0), axis=0
+        )
         piece_v = lax.all_gather(prior_v, "pipe", axis=0, tiled=True)
         count = piece_k.shape[0]
         fresh = partial_attend(

time: 787 us -> 548 us (0.70)
  waiting for transfers between devices: 670 us -> 382 us
  blocking collectives: 64.9 us -> 86.7 us
  starting transfers between devices: 0.42 us -> 20.7 us
  local copies, waits for them, and re-layouts: 8.75 us -> 17.5 us
    all_gather x2 -> x0, waiting for transfers between devices: 230 us -> none  [step(): piece_k = lax.all_gather(prior_k, 'pipe', axis=0, tiled=True)]
    all_gather x2, waiting for transfers between devices: 266 us -> 190 us  [step(): piece_v = lax.all_gather(prior_v, 'pipe', axis=0, tiled=True)]
    all_gather x2, blocking collectives: 64.9 us -> 86.7 us  [step(): lax.all_gather(x_rows, 'seq', axis=0, tiled=True)]
    all_to_all x0 -> x2, starting transfers between devices: none -> 20.3 us  [step(): lax.all_to_all(jnp.stack([prior_k] * lax.axis_size('pipe')), 'pipe', 0, 0)]
    all_to_all x0 -> x2, waiting for transfers between devices: none -> 17.9 us  [step(): lax.all_to_all(jnp.stack([prior_k] * lax.axis_size('pipe')), 'pipe', 0, 0)]
  transfers between devices with their start and end apart: 6 -> 6, of which waited for: 6 -> 5; matrix products, arithmetic and copies ran while one was open for 4% -> 7% of each run, Pallas kernels for 0% -> 0%
where the time goes in v1:
time: 548 us; the launch traced here: 547 us
  waiting for transfers between devices  382 us (70%)
  blocking collectives  86.7 us (16%)
  matrix products  22.8 us (4%)
  starting transfers between devices  20.7 us (4%)
  local copies, waits for them, and re-layouts  17.5 us (3%)
  between operations  14.1 us (3%)
    all_gather x2, waiting for transfers between devices, step(): piece_v = lax.all_gather(prior_v, 'pipe', axis=0, tiled=True)  190 us
    reduce_scatter x2, waiting for transfers between devices, step(): lax.psum_scatter(jnp.dot(attn, w_out, preferred_element_type=jnp.float32)...  173 us
    all_gather x2, blocking collectives, step(): lax.all_gather(x_rows, 'seq', axis=0, tiled=True)  86.7 us
    all_to_all x2, starting transfers between devices, step(): lax.all_to_all(jnp.stack([prior_k] * lax.axis_size('pipe')), 'pipe', 0, 0)  20.3 us
    all_to_all x2, waiting for transfers between devices, step(): lax.all_to_all(jnp.stack([prior_k] * lax.axis_size('pipe')), 'pipe', 0, 0)  17.9 us
    dot_general x4, matrix products, partial_attend(): jnp.einsum('hqk,khd->qhd', weights, values.astype(jnp.float32), precision...  12.9 us
  transfers between devices with their start and end apart: 6, of which 5 were waited for; matrix products, arithmetic and copies ran while one was open for 7% of the time, Pallas kernels for 0%

profile of v1, /device:TPU:8, one launch (start us, length us, event | category | flops | bytes accessed | tf_op | source)
XLA Modules:
  0.0 547.1 jit_solution(12383812722902590313)
XLA Ops:
  7.3 37.1 %all_gather.12 = bf16[128,2560]{1,0:T(8,128)(2,1)S(1)} all-gather(bf16[8,2560]{1,0:T(8,128)(2,1)} %param.10), channel_id=1, replica_groups=mesh['pipe'=32,'seq'=16] {'seq'}, dimensions={0}, use_global_device_ids=true | all-gather | bytes 696320 | tf_op jit(solution)/shard_map/all_gather | solution.py:80
  45.7 1.4 slice_bitcast_fusion
  47.2 1.2 stack.6
  48.5 10.7 %all-to-all-start = ((bf16[32,128,128]{1,2,0:T(8,128)(2,1)}), bf16[32,128,128]{1,2,0:T(8,128)(2,1)S(1)}, u32[]{:S(2)}, u32[]{:S(2)}) async-start(bf16[32,128,128]{1,2,0:T(8,128)(2,1)} %stack.6), calls=%async_computation | async-start | bytes 2097152 | tf_op jit(solution)/shard_map/all_to_all | solution.py:92
  60.3 49.6 %all_gather.14 = bf16[128,2560]{1,0:T(8,128)(2,1)S(1)} all-gather(bf16[8,2560]{1,0:T(8,128)(2,1)S(1)} %copy-done.5), channel_id=1, replica_groups=mesh['pipe'=32,'seq'=16] {'seq'}, dimensions={0}, use_global_device_ids=true | all-gather | bytes 696320 | tf_op jit(solution)/shard_map/all_gather | solution.py:80
  112.2 1.3 stack.8
  113.4 9.7 %all-to-all-start.1 = ((bf16[32,128,128]{1,2,0:T(8,128)(2,1)}), bf16[32,128,128]{1,2,0:T(8,128)(2,1)}, u32[]{:S(2)}, u32[]{:S(2)}) async-start(bf16[32,128,128]{1,2,0:T(8,128)(2,1)} %stack.8), calls=%async_computation.2 | async-start | bytes 2097152 | tf_op jit(solution)/shard_map/all_to_all | solution.py:92
  126.8 1.7 copy.32
  128.5 1.5 reshape_reshape.6
  130.1 2.8 fusion.61
  132.8 17.9 %all-to-all-done.1 = bf16[32,128,128]{1,2,0:T(8,128)(2,1)} async-done(((bf16[32,128,128]{1,2,0:T(8,128)(2,1)}), bf16[32,128,128]{1,2,0:T(8,128)(2,1)}, u32[]{:S(2)}, u32[]{:S(2)}) %all-to-all-start.1) | async-done | bytes 1048608 | tf_op jit(solution)/shard_map/all_to_all | solution.py:92
  150.7 2.9 copy.36
  153.6 1.5 reshape_reshape.7
  156.1 1.9 copy-done.2
  158.0 1.6 fusion.4
  159.7 52.6 %all-gather.7.cloned.1.call-done = bf16[1,4096,128]{1,2,0:T(8,128)(2,1)} async-done(((bf16[1,128,128]{1,2,0:T(8,128)(2,1)}), bf16[1,4096,128]{1,2,0:T(8,128)(2,1)}) %all-gather.7.cloned.1.call-update) | async-done | bytes 1048592 | tf_op jit(solution)/shard_map/all_gather | solution.py:94
  212.3 5.6 %fusion.23 = f32[128,2,64]{0,2,1:T(8,128)S(1)} fusion(bf16[4096,2,64]{0,2,1:T(8,128)(2,1)} %bitcast.123, f32[2,128,4096]{2,1,0:T(8,128)} %copy-done.1, f32[2,128]{1,0:T(2,128)S(1)} %get-tuple-element.18, pred[4096]{0:T(1024)(128)(4,1)S(1)} %broadcast_bitcast_fusion, f32[128,2]{0,1:T(2,128)S(1)} %get-tuple-element.6), kind=kOutput, calls=%fused_computation.35 | convolution fusion | flops 807419904 | bytes 5314560 | tf_op jit(solution)/shard_map/hqk,khd->qhd/dot_general | solution.py:47
  218.8 1.2 convolution_convert_fusion
  220.1 137.3 %all-gather.5.cloned.1.call-done = bf16[1,4096,128]{2,1,0:T(8,128)(2,1)} async-done(((bf16[1,128,128]{2,1,0:T(8,128)(2,1)}), bf16[1,4096,128]{2,1,0:T(8,128)(2,1)}) %all-gather.5.cloned.1.call-update) | async-done | bytes 1048592 | tf_op jit(solution)/shard_map/all_gather | solution.py:94
  357.4 2.3 copy.33
  359.7 5.5 %fusion.22 = f32[128,2,64]{0,2,1:T(8,128)S(1)} fusion(bf16[4096,2,64]{0,2,1:T(8,128)(2,1)} %bitcast.122, f32[2,128,4096]{2,1,0:T(8,128)} %get-tuple-element.17, f32[2,128]{1,0:T(2,128)S(1)} %get-tuple-element.16, pred[4096]{0:T(1024)(128)(4,1)S(1)} %broadcast_bitcast_fusion, f32[128,2]{0,1:T(2,128)S(1)} %get-tuple-element.9), kind=kOutput, calls=%fused_computation.34 | convolution fusion | flops 807419904 | bytes 5314560 | tf_op jit(solution)/shard_map/hqk,khd->qhd/dot_general | solution.py:47
  366.1 1.2 convolution_convert_fusion.1
  367.3 85.8 %reduce-scatter.5.cloned.1.call-done = bf16[8,2560]{1,0:T(8,128)(2,1)} async-done(((bf16[128,2560]{1,0:T(8,128)(2,1)}), bf16[8,2560]{1,0:T(8,128)(2,1)}) %reduce-scatter.5.cloned.1.call-update) | async-done | bytes 40976 | tf_op jit(solution)/shard_map/reduce_scatter | solution.py:106
  453.1 87.4 %reduce-scatter.3.cloned.1.call-done = bf16[8,2560]{1,0:T(8,128)(2,1)} async-done(((bf16[128,2560]{1,0:T(8,128)(2,1)}), bf16[8,2560]{1,0:T(8,128)(2,1)}) %reduce-scatter.3.cloned.1.call-update) | async-done | bytes 40976 | tf_op jit(solution)/shard_map/reduce_scatter | solution.py:106
  (66 shorter events, 11.3 us)
Async XLA Ops:
  7.2 37.2 %copy-start = (bf16[3,2560,128]{2,1,0:T(8,128)(2,1)S(1)}, bf16[3,2560,128]{2,1,0:T(8,128)(2,1)}, u32[]{:S(2)}) copy-start(bf16[3,2560,128]{2,1,0:T(8,128)(2,1)} %param.13) | copy-start | bytes 5898244
  7.2 52.7 %copy-start.6 = (s32[32,16]{0,1:T(8,128)S(1)}, s32[32,16]{0,1:T(8,128)}, u32[]{:S(2)}) copy-start(s32[32,16]{0,1:T(8,128)} %param.17) | copy-start | bytes 6148
  7.2 52.8 %copy-start.7 = (f32[128]{0:T(128)S(1)}, f32[128]{0:T(128)}, u32[]{:S(2)}) copy-start(f32[128]{0:T(128)} %param.16) | copy-start | bytes 1540
  7.2 53.0 %copy-start.10 = (f32[128]{0:T(128)S(1)}, f32[128]{0:T(128)}, u32[]{:S(2)}) copy-start(f32[128]{0:T(128)} %param.15) | copy-start | bytes 1540
  7.2 53.1 %copy-start.5 = (bf16[8,2560]{1,0:T(8,128)(2,1)S(1)}, bf16[8,2560]{1,0:T(8,128)(2,1)}, u32[]{:S(2)}) copy-start(bf16[8,2560]{1,0:T(8,128)(2,1)} %param.11) | copy-start | bytes 122884
  7.2 205.1 %all-gather.7.cloned.1.call-start = ((), (), s32[]{:S(2)}) async-start(), calls=%async_computation.7 | async-start | bytes 1081344 | tf_op jit(solution)/shard_map/all_gather | solution.py:94
  45.1 65.6 %copy-start.8 = (s32[32]{0:T(128)S(1)}, s32[32]{0:T(128)}, u32[]{:S(2)}) copy-start(s32[32]{0:T(128)} %param.18) | copy-start | bytes 388
  45.1 65.9 %copy-start.11 = (s32[32]{0:T(128)S(1)}, s32[32]{0:T(128)}, u32[]{:S(2)}) copy-start(s32[32]{0:T(128)} %param.19) | copy-start | bytes 388
  48.5 63.7 %all-to-all-start = ((bf16[32,128,128]{1,2,0:T(8,128)(2,1)}), bf16[32,128,128]{1,2,0:T(8,128)(2,1)S(1)}, u32[]{:S(2)}, u32[]{:S(2)}) async-start(bf16[32,128,128]{1,2,0:T(8,128)(2,1)} %stack.6), calls=%async_computation | async-start | bytes 2097152 | tf_op jit(solution)/shard_map/all_to_all | solution.py:92
  59.1 298.3 %all-gather.5.cloned.1.call-start = ((), (), s32[]{:S(2)}) async-start(), calls=%async_computation.6 | async-start | bytes 1081344 | tf_op jit(solution)/shard_map/all_gather | solution.py:94
  111.4 0.7 copy-start.9
  113.4 37.3 %all-to-all-start.1 = ((bf16[32,128,128]{1,2,0:T(8,128)(2,1)}), bf16[32,128,128]{1,2,0:T(8,128)(2,1)}, u32[]{:S(2)}, u32[]{:S(2)}) async-start(bf16[32,128,128]{1,2,0:T(8,128)(2,1)} %stack.8), calls=%async_computation.2 | async-start | bytes 2097152 | tf_op jit(solution)/shard_map/all_to_all | solution.py:92
  123.1 330.0 %reduce-scatter.5.cloned.1.call-start = ((), (), s32[]{:S(2)}) async-start(), calls=%async_computation.5 | async-start | bytes 696320 | tf_op jit(solution)/shard_map/reduce_scatter | solution.py:106
  155.1 2.9 copy-start.2
  156.1 3.6 copy-start.1
  159.7 59.1 %copy-start.3 = (bf16[128,2560]{1,0:T(8,128)(2,1)S(1)}, bf16[128,2560]{1,0:T(8,128)(2,1)}, u32[]{:S(2)}) copy-start(bf16[128,2560]{1,0:T(8,128)(2,1)} %param.14) | copy-start | bytes 1966084
  220.0 145.2 %copy-start.4 = (bf16[1,128,128]{1,2,0:T(8,128)(2,1)S(1)}, bf16[1,128,128]{1,2,0:T(8,128)(2,1)}, u32[]{:S(2)}) copy-start(bf16[1,128,128]{1,2,0:T(8,128)(2,1)} %slice.47) | copy-start | bytes 98308
  220.1 320.5 %reduce-scatter.3.cloned.1.call-start = ((), (), s32[]{:S(2)}) async-start(), calls=%async_computation.4 | async-start | bytes 696320 | tf_op jit(solution)/shard_map/reduce_scatter | solution.py:106
Sparse Core Ops, SparseCore 0:
  45.9 166.4 all-gather.6
  215.0 142.4 all-gather.4
  362.6 90.4 reduce-scatter.4
  458.2 82.3 reduce-scatter.2
